TPU v7x, 512 devices: a whole 4x8x8 slice. The times are simulated.
512 devices in a mesh: rows: 32 (over x, y_hi, core), cols: 16 (over z, y_lo).
Axes of the slice: x: 4, y: 8 (y_hi: 4, y_lo: 2; y = y_hi * 2 + y_lo), z: 8, core: 2. Of those that a mesh axis runs over, the one named last changes fastest.
Arguments:
- greens: bfloat16 [512, 262144], P('cols', 'rows'), may hold values from -0.5 to 0.5
- slip_values: bfloat16 [8192, 128], P('cols'), may hold values from 0.5 to 4
- rupture_ids: int32 [8192, 128], P('cols'), may hold values from -1 to 511, as said below
- win_point: int32 [4096], P('rows'), may hold values from 0 to 1023, never falling along the last dimension, each value on 1 to 32 neighbouring positions
Outputs:
- window_peak: float32 [8192, 4096], P('cols', 'rows')
Inputs may be any that keep to these rules, and one draw needn't show every extreme that they name: `rupture_ids`: each row lists its sources as one run of consecutive source numbers in its first slots and -1 in the rest; some row fills all 128 slots. `win_point`: never falls along the windows; every point holds 1 to 32 consecutive windows and some point exactly 32.
All inputs are finite; a program needn't handle non-finite values.
Results may differ from a plain program's by a relative error of at most 0.0003.
Values may be sent and summed in bfloat16 or wider, within the bound.
No kernel may reach another device: no remote copies, remote signals or barrier semaphores. Data moves between devices by JAX's collectives and lax.ppermute only.
A program may use at most 64 MiB of HBM per device.

v0:
```python
import jax
import jax.numpy as jnp
from jax import lax
from jax.sharding import Mesh
from jax.sharding import PartitionSpec as P

TSTEP = 64
COLS = ("cols_0", "cols_1")
SPLIT = "cols_0"
SHARE = "cols_1"


def extended(cells, sides, width):
    for axis, dim in sides:
        count = lax.axis_size(axis)
        ends = count - 1
        head = lax.slice_in_dim(cells, 0, width, axis=dim)
        tail = lax.slice_in_dim(cells, cells.shape[dim] - width, cells.shape[dim], axis=dim)
        cells = jnp.concatenate(
            [
                lax.ppermute(tail, axis, [(i, (i + 1) % count) for i in range(ends)]),
                cells,
                lax.ppermute(head, axis, [((i + 1) % count, i) for i in range(ends)]),
            ],
            axis=dim,
        )
    return cells


def shifted_slips(values, starts, width):
    count, slots = values.shape
    dense = jnp.concatenate([values, jnp.zeros((count, width - slots), values.dtype)], axis=1)
    bits = max(1, (width - 1).bit_length())
    for bit in range(bits):
        step = 1 << bit
        rolled = jnp.concatenate([dense[:, width - step :], dense[:, : width - step]], axis=1)
        dense = jnp.where((starts >> bit & 1)[:, None] == 1, rolled, dense)
    return dense


def combine(earlier, later):
    flag = jnp.logical_or(earlier[0], later[0])
    value = jnp.where(later[0], later[1], jnp.maximum(earlier[1], later[1]))
    return (flag, value)


def point_peaks(window_max, win_point):
    windows = window_max.shape[1]
    begins = jnp.concatenate([jnp.ones((1,), bool), win_point[1:] != win_point[:-1]])
    finals = jnp.concatenate([win_point[:-1] != win_point[1:], jnp.ones((1,), bool)])
    begin_flags = jnp.broadcast_to(begins[None, :], window_max.shape)
    final_flags = jnp.broadcast_to(finals[None, :], window_max.shape)
    forward = lax.associative_scan(combine, (begin_flags, window_max), axis=1)[1]
    backward = lax.associative_scan(combine, (final_flags, window_max), reverse=True, axis=1)[1]
    local_peak = jnp.maximum(forward, backward)
    edge_values = jnp.stack([backward[:, 0], forward[:, windows - 1]], axis=1)
    edge_points = jnp.stack([win_point[0] + 1, win_point[windows - 1] + 1]).astype(jnp.float32)[
        None, :
    ]
    padded_values, padded_points = (
        extended(edge_values, (("rows", 1),), 1),
        extended(edge_points, (("rows", 1),), 1),
    )
    point_code = (win_point + 1).astype(jnp.float32)[None, :]
    from_left = jnp.maximum(local_peak, padded_values[:, 0:1])
    local_peak = jnp.where(point_code == padded_points[0, 0], from_left, local_peak)
    from_right = jnp.maximum(local_peak, padded_values[:, 3:4])
    local_peak = jnp.where(point_code == padded_points[0, 3], from_right, local_peak)
    return local_peak


def local(greens, slip_values, rupture_ids, win_point):
    parts = lax.axis_size(SPLIT)
    shares = lax.axis_size(SHARE)
    own_sources, rows = greens.shape
    width = own_sources * parts * shares
    scen = slip_values.shape[0]
    block = rows // parts
    listed = rupture_ids >= 0
    values = jnp.where(listed, slip_values, jnp.zeros_like(slip_values))
    starts = jnp.maximum(rupture_ids[:, 0], 0)
    all_values = lax.all_gather(values, SPLIT, axis=0, tiled=True)
    all_starts = lax.all_gather(starts, SPLIT, axis=0, tiled=True)
    pieces = greens.reshape(own_sources, parts, block)
    pieces = lax.all_to_all(pieces, SPLIT, 1, 0, tiled=True)
    pieces = pieces.reshape(parts, own_sources, block)
    pieces = lax.all_gather(pieces, SHARE, axis=0, tiled=False)
    panel_t = jnp.transpose(pieces, (3, 1, 0, 2)).reshape(block, width)
    dense = shifted_slips(all_values, all_starts, width)
    wave_t = lax.dot_general(
        panel_t, dense, (((1,), (1,)), ((), ())), preferred_element_type=jnp.float32
    )
    win_block = block // TSTEP
    maxima = jnp.max(wave_t.reshape(win_block, TSTEP, parts * scen), axis=1)
    maxima = maxima.reshape(win_block, parts, scen)
    maxima = lax.all_to_all(maxima, SPLIT, 1, 0, tiled=True)
    window_max = maxima.reshape(parts * win_block, scen).T
    return point_peaks(window_max, win_point)


def solution(mesh):
    split = Mesh(mesh.devices.reshape(mesh.shape["rows"], 8, 2), ("rows", "cols_0", "cols_1"))
    in_specs = (P(COLS, "rows"), P(COLS, None), P(COLS, None), P("rows"))
    out_specs = P(COLS, "rows")
    return jax.shard_map(local, mesh=split, in_specs=in_specs, out_specs=out_specs, check_vma=False)
```

profile of v0, /device:TPU:21, one launch (start us, length us, event | category | flops | bytes accessed | tf_op | source)
XLA Modules:
  0.0 163.6 jit_solution(4431919119020084951)
XLA Ops:
  6.5 1.7 %compare_select_fusion = bf16[512,128]{1,0:T(8,128)(2,1)} fusion(bf16[512,128]{1,0:T(8,128)(2,1)} %param.5, s32[512,128]{1,0:T(8,128)} %param.6), kind=kLoop, calls=%fused_computation.38 | loop fusion | flops 131072 | bytes 524288 | tf_op jit(solution)/shard_map/jit(_where)/select_n | solution.py:80
  8.3 1.9 %copy.27 = bf16[4,8,8,1024]{3,2,0,1:T(8,128)(2,1)} copy(bf16[4,8,8,1024]{3,2,1,0:T(8,128)(2,1)} %bitcast.57) | data formatting | bytes 1048576 | tf_op jit(solution)/shard_map/reshape | solution.py:84
  10.2 10.0 %all-to-all-start = ((bf16[32,8,1024]{2,0,1:T(8,128)(2,1)}), bf16[32,8,1024]{2,0,1:T(8,128)(2,1)S(1)}, u32[]{:S(2)}, u32[]{:S(2)}) async-start(bf16[32,8,1024]{2,0,1:T(8,128)(2,1)} %bitcast.35), calls=%async_computation | async-start | bytes 1048576 | tf_op jit(solution)/shard_map/all_to_all | solution.py:85
  20.3 1.3 fusion.22
  22.8 1.0 slice_maximum_fusion
  23.8 40.5 %all-gather = s32[4096,1]{1,0:T(8,128)S(1)} all-gather(s32[512,1]{1,0:T(8,128)S(1)} %slice_maximum_fusion), channel_id=2, replica_groups=mesh['rows'=32,'cols_0'=8,'cols_1'=2] {'cols_0'}, dimensions={0}, use_global_device_ids=true | all-gather | bytes 18432 | tf_op jit(solution)/shard_map/all_gather | solution.py:83
  64.4 5.1 %fusion.4 = (pred[4096]{0:T(1024)(128)(4,1)S(1)}, pred[4096]{0:T(1024)(128)(4,1)S(1)}, pred[4096]{0:T(1024)(128)(4,1)S(1)}, pred[4096]{0:T(1024)(128)(4,1)S(1)},...) fusion(s32[4096,1]{1,0:T(8,128)S(1)} %all-gather), kind=kLoop, calls=%fused_computation.24 | loop fusion | flops 110592 | bytes 53248 | tf_op jit(solution)/shard_map/eq | solution.py:37
  69.4 0.8 copy-done.2
  70.3 1.7 %pad_slice_fusion = bf16[4096,511]{1,0:T(8,128)(2,1)S(1)} fusion(bf16[4096,128]{1,0:T(8,128)(2,1)} %all-gather.5.cloned.1.call-done), kind=kLoop, calls=%fused_computation.2 | loop fusion | bytes 5234688 | tf_op jit(solution)/shard_map/slice | solution.py:36
  72.0 4.1 %pad_select_fusion = bf16[4096,512]{1,0:T(8,128)(2,1)S(1)} fusion(bf16[4096,128]{1,0:T(8,128)(2,1)S(1)} %copy-done.1, bf16[4096,511]{1,0:T(8,128)(2,1)S(1)} %pad_slice_fusion, pred[4096]{0:T(1024)(128)(4,1)S(1)} %get-tuple-element.13), kind=kLoop, calls=%fused_computation.1 | loop fusion | flops 2097152 | bytes 9433088 | tf_op jit(solution)/shard_map/jit(_where)/select_n | solution.py:37
  76.4 4.0 %maximum_select_fusion = bf16[4096,512]{1,0:T(8,128)(2,1)S(1)} fusion(bf16[4096,512]{1,0:T(8,128)(2,1)S(1)} %pad_select_fusion, bf16[4096,510]{1,0:T(8,128)(2,1)S(1)} %bitcast.43, bf16[4096,2]{1,0:T(8,128)(2,1)S(1)} %slice.575, pred[4096]{0:T(1024)(128)(4,1)S(1)} %get-tuple-element.6), kind=kLoop, calls=%fused_computation.3 | loop fusion | flops 10485760 | bytes 12587008 | tf_op jit(solution)/shard_map/jit(_where)/select_n | solution.py:37
  80.8 4.0 %maximum_select_fusion.1 = bf16[4096,512]{1,0:T(8,128)(2,1)S(1)} fusion(bf16[4096,512]{1,0:T(8,128)(2,1)S(1)} %maximum_select_fusion, bf16[4096,508]{1,0:T(8,128)(2,1)S(1)} %bitcast.44, bf16[4096,4]{1,0:T(8,128)(2,1)S(1)} %slice.577, pred[4096]{0:T(1024)(128)(4,1)S(1)} %get-tuple-element.7), kind=kLoop, calls=%fused_computation.4 | loop fusion | flops 10485760 | bytes 12587008 | tf_op jit(solution)/shard_map/jit(_where)/select_n | solution.py:37
  85.2 4.0 %maximum_select_fusion.2 = bf16[4096,512]{1,0:T(8,128)(2,1)S(1)} fusion(bf16[4096,512]{1,0:T(8,128)(2,1)S(1)} %maximum_select_fusion.1, bf16[4096,504]{1,0:T(8,128)(2,1)S(1)} %bitcast.45, bf16[4096,8]{1,0:T(8,128)(2,1)S(1)} %slice.579, pred[4096]{0:T(1024)(128)(4,1)S(1)} %get-tuple-element.8), kind=kLoop, calls=%fused_computation.5 | loop fusion | flops 10485760 | bytes 12587008 | tf_op jit(solution)/shard_map/jit(_where)/select_n | solution.py:37
  89.6 4.0 %maximum_select_fusion.3 = bf16[4096,512]{1,0:T(8,128)(2,1)S(1)} fusion(bf16[4096,512]{1,0:T(8,128)(2,1)S(1)} %maximum_select_fusion.2, bf16[4096,496]{1,0:T(8,128)(2,1)S(1)} %bitcast.46, bf16[4096,16]{1,0:T(8,128)(2,1)S(1)} %slice.581, pred[4096]{0:T(1024)(128)(4,1)S(1)} %get-tuple-element.9), kind=kLoop, calls=%fused_computation.6 | loop fusion | flops 10485760 | bytes 12587008 | tf_op jit(solution)/shard_map/jit(_where)/select_n | solution.py:37
  94.0 4.0 %maximum_select_fusion.4 = bf16[4096,512]{1,0:T(8,128)(2,1)S(1)} fusion(bf16[4096,512]{1,0:T(8,128)(2,1)S(1)} %maximum_select_fusion.3, bf16[4096,480]{1,0:T(8,128)(2,1)S(1)} %bitcast.47, bf16[4096,32]{1,0:T(8,128)(2,1)S(1)} %slice.583, pred[4096]{0:T(1024)(128)(4,1)S(1)} %get-tuple-element.10), kind=kLoop, calls=%fused_computation.7 | loop fusion | flops 10485760 | bytes 12587008 | tf_op jit(solution)/shard_map/jit(_where)/select_n | solution.py:37
  98.4 4.2 %maximum_select_fusion.5 = bf16[4096,512]{1,0:T(8,128)(2,1)S(1)} fusion(bf16[4096,512]{1,0:T(8,128)(2,1)S(1)} %maximum_select_fusion.4, bf16[4096,448]{1,0:T(8,128)(2,1)S(1)} %bitcast.48, bf16[4096,64]{1,0:T(8,128)(2,1)S(1)} %slice.585, pred[4096]{0:T(1024)(128)(4,1)S(1)} %get-tuple-element.11), kind=kLoop, calls=%fused_computation.8 | loop fusion | flops 10485760 | bytes 12587008 | tf_op jit(solution)/shard_map/jit(_where)/select_n | solution.py:37
  103.1 2.2 %maximum_select_fusion.6 = bf16[4096,512]{1,0:T(8,128)(2,1)S(1)} fusion(bf16[4096,512]{1,0:T(8,128)(2,1)S(1)} %maximum_select_fusion.5, bf16[4096,384]{1,0:T(8,128)(2,1)S(1)} %slice.588, bf16[4096,128]{1,0:T(8,128)(2,1)S(1)} %slice.587, pred[4096]{0:T(1024)(128)(4,1)S(1)} %get-tuple-element.12), kind=kLoop, calls=%fused_computation.9 | loop fusion | flops 10485760 | bytes 12587008 | tf_op jit(solution)/shard_map/jit(_where)/select_n | solution.py:37
  105.4 1.9 %copy-done = bf16[4096,512]{1,0:T(8,128)(2,1)} copy-done((bf16[4096,512]{1,0:T(8,128)(2,1)}, bf16[4096,512]{1,0:T(8,128)(2,1)S(1)}, u32[]{:S(2)}) %copy-start) | copy-done | bytes 4194328
  107.3 1.6 fusion.17
  108.9 1.3 copy.20
  110.2 7.0 %bitcast_reduce_fusion = f32[16,4096]{1,0:T(8,128)S(1)} fusion(bf16[1024,512]{0,1:T(8,128)(2,1)S(1)} %bitcast.56, bf16[4096,512]{1,0:T(8,128)(2,1)} %copy-done, bf16[4096,256]{1,0:T(8,128)(2,1)} %get-tuple-element.15, bf16[4096,256]{1,0:T(8,128)(2,1)S(1)} %get-tuple-element.14, pred[4096]{0:T(1024)(128)(4,1)S(1)} %get-tuple-element.5), kind=kOutput, calls=%fused_computation | convolution fusion | flops 4309581824 | bytes 9703424 | tf_op jit(solution)/shard_map/dot_general | solution.py:90
  117.2 0.7 copy.28
  118.0 5.1 %all-to-all-start.1 = ((f32[16,8,512]{2,0,1:T(8,128)}), f32[16,8,512]{2,0,1:T(8,128)S(1)}, u32[]{:S(2)}, u32[]{:S(2)}) async-start(f32[16,8,512]{2,0,1:T(8,128)} %bitcast.36), calls=%async_computation.1 | async-start | bytes 524288 | tf_op jit(solution)/shard_map/all_to_all | solution.py:96
  123.6 7.0 %collective-permute-start = (f32[1,1]{1,0:T(1,128)}, f32[1,1]{1,0:T(1,128)}, u32[]{:S(2)}, u32[]{:S(2)}) collective-permute-start(f32[1,1]{1,0:T(1,128)} %get-tuple-element.28), channel_id=1, source_target_pairs={{16,0},{32,16},{48,32},{64,48},{80,64},{96,80},{112,96},{128,112},... | collective-permute-start | bytes 20 | tf_op jit(solution)/shard_map/ppermute | solution.py:23
  130.6 5.1 %collective-permute-start.1 = (f32[1,1]{1,0:T(1,128)}, f32[1,1]{1,0:T(1,128)}, u32[]{:S(2)}, u32[]{:S(2)}) collective-permute-start(f32[1,1]{1,0:T(1,128)} %get-tuple-element.29), channel_id=1, source_target_pairs={{0,16},{16,32},{32,48},{48,64},{64,80},{80,96},{96,112},{112,128},... | collective-permute-start | bytes 20 | tf_op jit(solution)/shard_map/ppermute | solution.py:21
  137.4 0.6 slice.501
  143.4 0.6 broadcast_select_fusion
  145.5 2.6 %collective-permute-start.2 = (f32[512,1]{0,1:T(1,128)S(1)}, f32[512,1]{0,1:T(1,128)S(1)}, u32[]{:S(2)}, u32[]{:S(2)}) collective-permute-start(f32[512,1]{0,1:T(1,128)S(1)} %slice_add_fusion.1), channel_id=1, source_target_pairs={{0,16},{16,32},{32,48},{48,64},{64,80},{80,96},{96,112},{112,128},... | collective-permute-start | bytes 6152 | tf_op jit(solution)/shard_map/ppermute | solution.py:21
  148.8 1.9 %collective-permute-start.3 = (f32[512,1]{0,1:T(1,128)S(1)}, f32[512,1]{0,1:T(1,128)S(1)}, u32[]{:S(2)}, u32[]{:S(2)}) collective-permute-start(f32[512,1]{0,1:T(1,128)S(1)} %slice_add_fusion), channel_id=1, source_target_pairs={{16,0},{32,16},{48,32},{64,48},{80,64},{96,80},{112,96},{128,112},... | collective-permute-start | bytes 6152 | tf_op jit(solution)/shard_map/ppermute | solution.py:23
  150.8 1.3 convert_compare_fusion.1
  152.3 3.6 %collective-permute-done.3 = f32[512,1]{0,1:T(1,128)S(1)} collective-permute-done((f32[512,1]{0,1:T(1,128)S(1)}, f32[512,1]{0,1:T(1,128)S(1)}, u32[]{:S(2)}, u32[]{:S(2)}) %collective-permute-start.3) | collective-permute-done | bytes 2080 | tf_op jit(solution)/shard_map/ppermute | solution.py:23
  156.0 0.8 copy.22
  (204 shorter events, 12.2 us)
Async XLA Ops:
  6.5 63.7 %all-gather.5.cloned.1.call-start = ((), (), s32[]{:S(2)}) async-start(), calls=%async_computation.2 | async-start | bytes 1179648 | tf_op jit(solution)/shard_map/all_gather | solution.py:82
  10.2 59.3 %all-to-all-start = ((bf16[32,8,1024]{2,0,1:T(8,128)(2,1)}), bf16[32,8,1024]{2,0,1:T(8,128)(2,1)S(1)}, u32[]{:S(2)}, u32[]{:S(2)}) async-start(bf16[32,8,1024]{2,0,1:T(8,128)(2,1)} %bitcast.35), calls=%async_computation | async-start | bytes 1048576 | tf_op jit(solution)/shard_map/all_to_all | solution.py:85
  20.2 88.7 %all-gather.7.cloned.1.call-start = ((), (), s32[]{:S(2)}) async-start(), calls=%async_computation.3 | async-start | bytes 1572864 | tf_op jit(solution)/shard_map/all_gather | solution.py:87
  69.4 0.8 copy-start.2
  70.3 1.7 %copy-start.1 = (bf16[4096,128]{1,0:T(8,128)(2,1)S(1)}, bf16[4096,128]{1,0:T(8,128)(2,1)}, u32[]{:S(2)}) copy-start(bf16[4096,128]{1,0:T(8,128)(2,1)} %all-gather.5.cloned.1.call-done) | copy-start | bytes 3145732
  105.4 1.9 %copy-start = (bf16[4096,512]{1,0:T(8,128)(2,1)}, bf16[4096,512]{1,0:T(8,128)(2,1)S(1)}, u32[]{:S(2)}) copy-start(bf16[4096,512]{1,0:T(8,128)(2,1)S(1)} %maximum_select_fusion.6) | copy-start | bytes 12582916
  110.2 25.6 %copy-start.3 = (s32[128]{0:T(128)S(1)}, s32[128]{0:T(128)}, u32[]{:S(2)}) copy-start(s32[128]{0:T(128)} %param.7) | copy-start | bytes 1540
  118.0 23.2 %all-to-all-start.1 = ((f32[16,8,512]{2,0,1:T(8,128)}), f32[16,8,512]{2,0,1:T(8,128)S(1)}, u32[]{:S(2)}, u32[]{:S(2)}) async-start(f32[16,8,512]{2,0,1:T(8,128)} %bitcast.36), calls=%async_computation.1 | async-start | bytes 524288 | tf_op jit(solution)/shard_map/all_to_all | solution.py:96
  123.6 27.2 %collective-permute-start = (f32[1,1]{1,0:T(1,128)}, f32[1,1]{1,0:T(1,128)}, u32[]{:S(2)}, u32[]{:S(2)}) collective-permute-start(f32[1,1]{1,0:T(1,128)} %get-tuple-element.28), channel_id=1, source_target_pairs={{16,0},{32,16},{48,32},{64,48},{80,64},{96,80},{112,96},{128,112},... | collective-permute-start | bytes 20 | tf_op jit(solution)/shard_map/ppermute | solution.py:23
  130.6 20.1 %collective-permute-start.1 = (f32[1,1]{1,0:T(1,128)}, f32[1,1]{1,0:T(1,128)}, u32[]{:S(2)}, u32[]{:S(2)}) collective-permute-start(f32[1,1]{1,0:T(1,128)} %get-tuple-element.29), channel_id=1, source_target_pairs={{0,16},{16,32},{32,48},{48,64},{64,80},{80,96},{96,112},{112,128},... | collective-permute-start | bytes 20 | tf_op jit(solution)/shard_map/ppermute | solution.py:21
  145.5 6.8 %collective-permute-start.2 = (f32[512,1]{0,1:T(1,128)S(1)}, f32[512,1]{0,1:T(1,128)S(1)}, u32[]{:S(2)}, u32[]{:S(2)}) collective-permute-start(f32[512,1]{0,1:T(1,128)S(1)} %slice_add_fusion.1), channel_id=1, source_target_pairs={{0,16},{16,32},{32,48},{48,64},{64,80},{80,96},{96,112},{112,128},... | collective-permute-start | bytes 6152 | tf_op jit(solution)/shard_map/ppermute | solution.py:21
  148.8 7.0 %collective-permute-start.3 = (f32[512,1]{0,1:T(1,128)S(1)}, f32[512,1]{0,1:T(1,128)S(1)}, u32[]{:S(2)}, u32[]{:S(2)}) collective-permute-start(f32[512,1]{0,1:T(1,128)S(1)} %slice_add_fusion), channel_id=1, source_target_pairs={{16,0},{32,16},{48,32},{64,48},{80,64},{96,80},{112,96},{128,112},... | collective-permute-start | bytes 6152 | tf_op jit(solution)/shard_map/ppermute | solution.py:23
Sparse Core Ops, SparseCore 0:
  9.4 47.3 all-gather.4
  70.4 32.4 all-gather.6
where the time goes:
time: 164 us
  other arithmetic  42.9 us (26%)
  blocking collectives  40.5 us (25%)
  starting transfers between devices  31.8 us (19%)
  local copies, waits for them, and re-layouts  22.3 us (14%)
  between operations  15.6 us (10%)
  matrix products  6.99 us (4%)
  waiting for transfers between devices  3.65 us (2%)
    all_gather x1, blocking collectives, local(): all_starts = lax.all_gather(starts, SPLIT, axis=0, tiled=True)  40.5 us
    select_n x8, other arithmetic, shifted_slips(): dense = jnp.where((starts >> bit & 1)[:, None] == 1, rolled, dense)  30.8 us
    all_to_all x1, starting transfers between devices, local(): pieces = lax.all_to_all(pieces, SPLIT, 1, 0, tiled=True)  10 us
    ppermute x2, starting transfers between devices, extended(): lax.ppermute(head, axis, [((i + 1) % count, i) for i in range(ends)])  8.94 us
    ppermute x2, starting transfers between devices, extended(): lax.ppermute(tail, axis, [(i, (i + 1) % count) for i in range(ends)])  7.7 us
    dot_general x1, matrix products, local(): lax.dot_general(panel_t, dense, (((1,), (1,)), ((), ())), preferred_eleme...  6.99 us
    eq x1, other arithmetic, shifted_slips(): dense = jnp.where((starts >> bit & 1)[:, None] == 1, rolled, dense)  5.06 us
    all_to_all x1, starting transfers between devices, local(): maxima = lax.all_to_all(maxima, SPLIT, 1, 0, tiled=True)  5.05 us
  transfers between devices with their start and end apart: 8, of which 1 were waited for; matrix products, arithmetic and copies ran while one was open for 35% of the time, Pallas kernels for 0%

commit v1 on v0

--- a/solution.py
+++ b/solution.py
@@ -80,7 +80,10 @@
     values = jnp.where(listed, slip_values, jnp.zeros_like(slip_values))
     starts = jnp.maximum(rupture_ids[:, 0], 0)
     all_values = lax.all_gather(values, SPLIT, axis=0, tiled=True)
-    all_starts = lax.all_gather(starts, SPLIT, axis=0, tiled=True)
+    _attach_vector = lambda panel, chip_axis: jnp.concatenate(
+        lax.all_to_all(jnp.stack(lax.axis_size(chip_axis) * [panel], 0), chip_axis, 0, 0), 0
+    )
+    all_starts = _attach_vector(starts, SPLIT)
     pieces = greens.reshape(own_sources, parts, block)
     pieces = lax.all_to_all(pieces, SPLIT, 1, 0, tiled=True)
     pieces = pieces.reshape(parts, own_sources, block)

time: 164 us -> 149 us (0.909)
  the two profiles are of different devices: /device:TPU:21 before, /device:TPU:23 now
where the time goes in v1:
time: 149 us; the launch traced here: 148 us
  other arithmetic  38.3 us (26%)
  starting transfers between devices  33.7 us (23%)
  waiting for transfers between devices  30.4 us (20%)
  local copies, waits for them, and re-layouts  23 us (15%)
  between operations  15.6 us (10%)
  matrix products  7.17 us (5%)
    select_n x8, other arithmetic, shifted_slips(): dense = jnp.where((starts >> bit & 1)[:, None] == 1, rolled, dense)  30.6 us
    all_to_all x1, waiting for transfers between devices, local(): pieces = lax.all_to_all(pieces, SPLIT, 1, 0, tiled=True)  17.4 us
    all_to_all x1, starting transfers between devices, local(): lax.all_to_all(jnp.stack(lax.axis_size(chip_axis) * [panel], 0), chip_axi...  10 us
    ppermute x2, starting transfers between devices, extended(): lax.ppermute(head, axis, [((i + 1) % count, i) for i in range(ends)])  7.91 us
    ppermute x2, starting transfers between devices, extended(): lax.ppermute(tail, axis, [(i, (i + 1) % count) for i in range(ends)])  7.69 us
    dot_general x1, matrix products, local(): lax.dot_general(panel_t, dense, (((1,), (1,)), ((), ())), preferred_eleme...  7.17 us
    all_to_all x1, waiting for transfers between devices, local(): lax.all_to_all(jnp.stack(lax.axis_size(chip_axis) * [panel], 0), chip_axi...  4.72 us
    all_gather x1, waiting for transfers between devices, local(): all_values = lax.all_gather(values, SPLIT, axis=0, tiled=True)  4.62 us
  transfers between devices with their start and end apart: 9, of which 4 were waited for; matrix products, arithmetic and copies ran while one was open for 36% of the time, Pallas kernels for 0%

profile of v1, /device:TPU:23, one launch (start us, length us, event | category | flops | bytes accessed | tf_op | source)
XLA Modules:
  0.0 148.1 jit_solution(9590646941835409951)
XLA Ops:
  6.5 1.7 %compare_select_fusion = bf16[512,128]{1,0:T(8,128)(2,1)} fusion(bf16[512,128]{1,0:T(8,128)(2,1)} %param.5, s32[512,128]{1,0:T(8,128)} %param.6), kind=kLoop, calls=%fused_computation.20 | loop fusion | flops 131072 | bytes 524288 | tf_op jit(solution)/shard_map/jit(_where)/select_n | solution.py:80
  8.3 1.1 maximum_reduce_fusion
  10.0 10.0 %all-to-all-start = ((s32[8,1,512]{2,1,0:T(1,128)}), s32[8,1,512]{2,1,0:T(1,128)S(1)}, u32[]{:S(2)}, u32[]{:S(2)}) async-start(s32[8,1,512]{2,1,0:T(1,128)} %stack.11), calls=%async_computation | async-start | bytes 32768 | tf_op jit(solution)/shard_map/all_to_all | solution.py:84
  20.0 1.9 %copy.36 = bf16[4,8,8,1024]{3,2,0,1:T(8,128)(2,1)} copy(bf16[4,8,8,1024]{3,2,1,0:T(8,128)(2,1)} %bitcast.75) | data formatting | bytes 1048576 | tf_op jit(solution)/shard_map/reshape | solution.py:87
  21.9 4.7 %all-to-all-done = s32[8,1,512]{2,1,0:T(1,128)S(1)} async-done(((s32[8,1,512]{2,1,0:T(1,128)}), s32[8,1,512]{2,1,0:T(1,128)S(1)}, u32[]{:S(2)}, u32[]{:S(2)}) %all-to-all-start) | async-done | bytes 16416 | tf_op jit(solution)/shard_map/all_to_all | solution.py:84
  26.6 3.5 %all-to-all-start.1 = ((bf16[32,8,1024]{2,0,1:T(8,128)(2,1)}), bf16[32,8,1024]{2,0,1:T(8,128)(2,1)S(1)}, u32[]{:S(2)}, u32[]{:S(2)}) async-start(bf16[32,8,1024]{2,0,1:T(8,128)(2,1)} %bitcast.53), calls=%async_computation.1 | async-start | bytes 1048576 | tf_op jit(solution)/shard_map/all_to_all | solution.py:88
  30.2 1.3 fusion.13
  33.5 17.4 %all-to-all-done.1 = bf16[32,8,1024]{2,0,1:T(8,128)(2,1)S(1)} async-done(((bf16[32,8,1024]{2,0,1:T(8,128)(2,1)}), bf16[32,8,1024]{2,0,1:T(8,128)(2,1)S(1)}, u32[]{:S(2)}, u32[]{:S(2)}) %all-to-all-start.1) | async-done | bytes 524320 | tf_op jit(solution)/shard_map/all_to_all | solution.py:88
  50.9 0.8 copy-done.2
  51.7 4.6 %all-gather.4.cloned.1.call-done = bf16[4096,128]{1,0:T(8,128)(2,1)} async-done(((bf16[512,128]{1,0:T(8,128)(2,1)}), bf16[4096,128]{1,0:T(8,128)(2,1)}) %all-gather.4.cloned.1.call-update) | async-done | bytes 1048592 | tf_op jit(solution)/shard_map/all_gather | solution.py:82
  56.3 1.7 %pad_slice_fusion = bf16[4096,511]{1,0:T(8,128)(2,1)S(1)} fusion(bf16[4096,128]{1,0:T(8,128)(2,1)} %all-gather.4.cloned.1.call-done), kind=kLoop, calls=%fused_computation.2 | loop fusion | bytes 5234688 | tf_op jit(solution)/shard_map/slice | solution.py:36
  58.0 4.1 %pad_select_fusion = bf16[4096,512]{1,0:T(8,128)(2,1)S(1)} fusion(bf16[4096,128]{1,0:T(8,128)(2,1)S(1)} %copy-done.1, bf16[4096,511]{1,0:T(8,128)(2,1)S(1)} %pad_slice_fusion, pred[4096]{0:T(1024)(128)(4,1)S(1)} %bitcast.84), kind=kLoop, calls=%fused_computation.1 | loop fusion | flops 2097152 | bytes 9433088 | tf_op jit(solution)/shard_map/jit(_where)/select_n | solution.py:37
  62.5 4.0 %maximum_select_fusion = bf16[4096,512]{1,0:T(8,128)(2,1)S(1)} fusion(bf16[4096,512]{1,0:T(8,128)(2,1)S(1)} %pad_select_fusion, bf16[4096,510]{1,0:T(8,128)(2,1)S(1)} %bitcast.61, bf16[4096,2]{1,0:T(8,128)(2,1)S(1)} %slice.575, pred[4096]{0:T(1024)(128)(4,1)S(1)} %bitcast.82), kind=kLoop, calls=%fused_computation.3 | loop fusion | flops 10485760 | bytes 12587008 | tf_op jit(solution)/shard_map/jit(_where)/select_n | solution.py:37
  66.9 4.0 %maximum_select_fusion.1 = bf16[4096,512]{1,0:T(8,128)(2,1)S(1)} fusion(bf16[4096,512]{1,0:T(8,128)(2,1)S(1)} %maximum_select_fusion, bf16[4096,508]{1,0:T(8,128)(2,1)S(1)} %bitcast.62, bf16[4096,4]{1,0:T(8,128)(2,1)S(1)} %slice.577, pred[4096]{0:T(1024)(128)(4,1)S(1)} %bitcast.81), kind=kLoop, calls=%fused_computation.4 | loop fusion | flops 10485760 | bytes 12587008 | tf_op jit(solution)/shard_map/jit(_where)/select_n | solution.py:37
  71.3 4.0 %maximum_select_fusion.2 = bf16[4096,512]{1,0:T(8,128)(2,1)S(1)} fusion(bf16[4096,512]{1,0:T(8,128)(2,1)S(1)} %maximum_select_fusion.1, bf16[4096,504]{1,0:T(8,128)(2,1)S(1)} %bitcast.63, bf16[4096,8]{1,0:T(8,128)(2,1)S(1)} %slice.579, pred[4096]{0:T(1024)(128)(4,1)S(1)} %bitcast.80), kind=kLoop, calls=%fused_computation.5 | loop fusion | flops 10485760 | bytes 12587008 | tf_op jit(solution)/shard_map/jit(_where)/select_n | solution.py:37
  75.7 4.0 %maximum_select_fusion.3 = bf16[4096,512]{1,0:T(8,128)(2,1)S(1)} fusion(bf16[4096,512]{1,0:T(8,128)(2,1)S(1)} %maximum_select_fusion.2, bf16[4096,496]{1,0:T(8,128)(2,1)S(1)} %bitcast.64, bf16[4096,16]{1,0:T(8,128)(2,1)S(1)} %slice.581, pred[4096]{0:T(1024)(128)(4,1)S(1)} %bitcast.79), kind=kLoop, calls=%fused_computation.6 | loop fusion | flops 10485760 | bytes 12587008 | tf_op jit(solution)/shard_map/jit(_where)/select_n | solution.py:37
  80.1 4.0 %maximum_select_fusion.4 = bf16[4096,512]{1,0:T(8,128)(2,1)S(1)} fusion(bf16[4096,512]{1,0:T(8,128)(2,1)S(1)} %maximum_select_fusion.3, bf16[4096,480]{1,0:T(8,128)(2,1)S(1)} %bitcast.65, bf16[4096,32]{1,0:T(8,128)(2,1)S(1)} %slice.583, pred[4096]{0:T(1024)(128)(4,1)S(1)} %bitcast.78), kind=kLoop, calls=%fused_computation.7 | loop fusion | flops 10485760 | bytes 12587008 | tf_op jit(solution)/shard_map/jit(_where)/select_n | solution.py:37
  84.5 4.0 %maximum_select_fusion.5 = bf16[4096,512]{1,0:T(8,128)(2,1)S(1)} fusion(bf16[4096,512]{1,0:T(8,128)(2,1)S(1)} %maximum_select_fusion.4, bf16[4096,448]{1,0:T(8,128)(2,1)S(1)} %bitcast.66, bf16[4096,64]{1,0:T(8,128)(2,1)S(1)} %slice.585, pred[4096]{0:T(1024)(128)(4,1)S(1)} %bitcast.77), kind=kLoop, calls=%fused_computation.8 | loop fusion | flops 10485760 | bytes 12587008 | tf_op jit(solution)/shard_map/jit(_where)/select_n | solution.py:37
  89.0 2.2 %maximum_select_fusion.6 = bf16[4096,512]{1,0:T(8,128)(2,1)S(1)} fusion(bf16[4096,512]{1,0:T(8,128)(2,1)S(1)} %maximum_select_fusion.5, bf16[4096,384]{1,0:T(8,128)(2,1)S(1)} %slice.588, bf16[4096,128]{1,0:T(8,128)(2,1)S(1)} %slice.587, pred[4096]{0:T(1024)(128)(4,1)S(1)} %bitcast.83), kind=kLoop, calls=%fused_computation.9 | loop fusion | flops 10485760 | bytes 12587008 | tf_op jit(solution)/shard_map/jit(_where)/select_n | solution.py:37
  91.3 1.9 %copy-done = bf16[4096,512]{1,0:T(8,128)(2,1)} copy-done((bf16[4096,512]{1,0:T(8,128)(2,1)}, bf16[4096,512]{1,0:T(8,128)(2,1)S(1)}, u32[]{:S(2)}) %copy-start) | copy-done | bytes 4194328
  93.2 1.6 %fusion.8 = (bf16[4096,256]{1,0:T(8,128)(2,1)S(1)}, bf16[4096,256]{1,0:T(8,128)(2,1)}) fusion(bf16[4096,512]{1,0:T(8,128)(2,1)S(1)} %maximum_select_fusion.6), kind=kLoop, calls=%fused_computation.87 | loop fusion | bytes 8388608 | tf_op jit(solution)/shard_map/slice | solution.py:36
  94.8 1.3 copy.20
  96.1 7.2 %bitcast_reduce_fusion = f32[16,4096]{1,0:T(8,128)S(1)} fusion(bf16[1024,512]{0,1:T(8,128)(2,1)S(1)} %bitcast.74, bf16[4096,512]{1,0:T(8,128)(2,1)} %copy-done, bf16[4096,256]{1,0:T(8,128)(2,1)} %get-tuple-element.15, bf16[4096,256]{1,0:T(8,128)(2,1)S(1)} %get-tuple-element.14, pred[4096]{0:T(1024)(128)(4,1)S(1)} %bitcast.94), kind=kOutput, calls=%fused_computation | convolution fusion | flops 4309581824 | bytes 9703424 | tf_op jit(solution)/shard_map/dot_general | solution.py:93
  103.3 0.7 copy.37
  104.0 4.5 %all-to-all-start.2 = ((f32[16,8,512]{2,0,1:T(8,128)}), f32[16,8,512]{2,0,1:T(8,128)S(1)}, u32[]{:S(2)}, u32[]{:S(2)}) async-start(f32[16,8,512]{2,0,1:T(8,128)} %bitcast.54), calls=%async_computation.2 | async-start | bytes 524288 | tf_op jit(solution)/shard_map/all_to_all | solution.py:99
  109.1 6.0 %collective-permute-start = (f32[1,1]{1,0:T(1,128)}, f32[1,1]{1,0:T(1,128)}, u32[]{:S(2)}, u32[]{:S(2)}) collective-permute-start(f32[1,1]{1,0:T(1,128)} %get-tuple-element.28), channel_id=1, source_target_pairs={{16,0},{32,16},{48,32},{64,48},{80,64},{96,80},{112,96},{128,112},... | collective-permute-start | bytes 20 | tf_op jit(solution)/shard_map/ppermute | solution.py:23
  115.1 5.1 %collective-permute-start.1 = (f32[1,1]{1,0:T(1,128)}, f32[1,1]{1,0:T(1,128)}, u32[]{:S(2)}, u32[]{:S(2)}) collective-permute-start(f32[1,1]{1,0:T(1,128)} %get-tuple-element.29), channel_id=1, source_target_pairs={{0,16},{16,32},{32,48},{48,64},{64,80},{80,96},{96,112},{112,128},... | collective-permute-start | bytes 20 | tf_op jit(solution)/shard_map/ppermute | solution.py:21
  129.9 2.6 %collective-permute-start.2 = (f32[512,1]{0,1:T(1,128)S(1)}, f32[512,1]{0,1:T(1,128)S(1)}, u32[]{:S(2)}, u32[]{:S(2)}) collective-permute-start(f32[512,1]{0,1:T(1,128)S(1)} %slice_add_fusion.1), channel_id=1, source_target_pairs={{0,16},{16,32},{32,48},{48,64},{64,80},{80,96},{96,112},{112,128},... | collective-permute-start | bytes 6152 | tf_op jit(solution)/shard_map/ppermute | solution.py:21
  133.3 1.9 %collective-permute-start.3 = (f32[512,1]{0,1:T(1,128)S(1)}, f32[512,1]{0,1:T(1,128)S(1)}, u32[]{:S(2)}, u32[]{:S(2)}) collective-permute-start(f32[512,1]{0,1:T(1,128)S(1)} %slice_add_fusion), channel_id=1, source_target_pairs={{16,0},{32,16},{48,32},{64,48},{80,64},{96,80},{112,96},{128,112},... | collective-permute-start | bytes 6152 | tf_op jit(solution)/shard_map/ppermute | solution.py:23
  135.2 1.3 convert_compare_fusion.1
  136.7 3.6 %collective-permute-done.3 = f32[512,1]{0,1:T(1,128)S(1)} collective-permute-done((f32[512,1]{0,1:T(1,128)S(1)}, f32[512,1]{0,1:T(1,128)S(1)}, u32[]{:S(2)}, u32[]{:S(2)}) %collective-permute-start.3) | collective-permute-done | bytes 2080 | tf_op jit(solution)/shard_map/ppermute | solution.py:23
  140.4 0.8 copy.22
  (215 shorter events, 14.6 us)
Async XLA Ops:
  6.5 49.8 %all-gather.4.cloned.1.call-start = ((), (), s32[]{:S(2)}) async-start(), calls=%async_computation.3 | async-start | bytes 1179648 | tf_op jit(solution)/shard_map/all_gather | solution.py:82
  10.0 16.7 %all-to-all-start = ((s32[8,1,512]{2,1,0:T(1,128)}), s32[8,1,512]{2,1,0:T(1,128)S(1)}, u32[]{:S(2)}, u32[]{:S(2)}) async-start(s32[8,1,512]{2,1,0:T(1,128)} %stack.11), calls=%async_computation | async-start | bytes 32768 | tf_op jit(solution)/shard_map/all_to_all | solution.py:84
  26.6 24.3 %all-to-all-start.1 = ((bf16[32,8,1024]{2,0,1:T(8,128)(2,1)}), bf16[32,8,1024]{2,0,1:T(8,128)(2,1)S(1)}, u32[]{:S(2)}, u32[]{:S(2)}) async-start(bf16[32,8,1024]{2,0,1:T(8,128)(2,1)} %bitcast.53), calls=%async_computation.1 | async-start | bytes 1048576 | tf_op jit(solution)/shard_map/all_to_all | solution.py:88
  30.1 64.6 %all-gather.6.cloned.1.call-start = ((), (), s32[]{:S(2)}) async-start(), calls=%async_computation.4 | async-start | bytes 1572864 | tf_op jit(solution)/shard_map/all_gather | solution.py:90
  50.9 0.8 copy-start.2
  56.3 1.7 %copy-start.1 = (bf16[4096,128]{1,0:T(8,128)(2,1)S(1)}, bf16[4096,128]{1,0:T(8,128)(2,1)}, u32[]{:S(2)}) copy-start(bf16[4096,128]{1,0:T(8,128)(2,1)} %all-gather.4.cloned.1.call-done) | copy-start | bytes 3145732
  91.3 1.9 %copy-start = (bf16[4096,512]{1,0:T(8,128)(2,1)}, bf16[4096,512]{1,0:T(8,128)(2,1)S(1)}, u32[]{:S(2)}) copy-start(bf16[4096,512]{1,0:T(8,128)(2,1)S(1)} %maximum_select_fusion.6) | copy-start | bytes 12582916
  96.1 24.1 %copy-start.3 = (s32[128]{0:T(128)S(1)}, s32[128]{0:T(128)}, u32[]{:S(2)}) copy-start(s32[128]{0:T(128)} %param.7) | copy-start | bytes 1540
  104.0 21.6 %all-to-all-start.2 = ((f32[16,8,512]{2,0,1:T(8,128)}), f32[16,8,512]{2,0,1:T(8,128)S(1)}, u32[]{:S(2)}, u32[]{:S(2)}) async-start(f32[16,8,512]{2,0,1:T(8,128)} %bitcast.54), calls=%async_computation.2 | async-start | bytes 524288 | tf_op jit(solution)/shard_map/all_to_all | solution.py:99
  109.1 26.1 %collective-permute-start = (f32[1,1]{1,0:T(1,128)}, f32[1,1]{1,0:T(1,128)}, u32[]{:S(2)}, u32[]{:S(2)}) collective-permute-start(f32[1,1]{1,0:T(1,128)} %get-tuple-element.28), channel_id=1, source_target_pairs={{16,0},{32,16},{48,32},{64,48},{80,64},{96,80},{112,96},{128,112},... | collective-permute-start | bytes 20 | tf_op jit(solution)/shard_map/ppermute | solution.py:23
  115.1 20.1 %collective-permute-start.1 = (f32[1,1]{1,0:T(1,128)}, f32[1,1]{1,0:T(1,128)}, u32[]{:S(2)}, u32[]{:S(2)}) collective-permute-start(f32[1,1]{1,0:T(1,128)} %get-tuple-element.29), channel_id=1, source_target_pairs={{0,16},{16,32},{32,48},{48,64},{64,80},{80,96},{96,112},{112,128},... | collective-permute-start | bytes 20 | tf_op jit(solution)/shard_map/ppermute | solution.py:21
  129.9 6.8 %collective-permute-start.2 = (f32[512,1]{0,1:T(1,128)S(1)}, f32[512,1]{0,1:T(1,128)S(1)}, u32[]{:S(2)}, u32[]{:S(2)}) collective-permute-start(f32[512,1]{0,1:T(1,128)S(1)} %slice_add_fusion.1), channel_id=1, source_target_pairs={{0,16},{16,32},{32,48},{48,64},{64,80},{80,96},{96,112},{112,128},... | collective-permute-start | bytes 6152 | tf_op jit(solution)/shard_map/ppermute | solution.py:21
  133.3 7.0 %collective-permute-start.3 = (f32[512,1]{0,1:T(1,128)S(1)}, f32[512,1]{0,1:T(1,128)S(1)}, u32[]{:S(2)}, u32[]{:S(2)}) collective-permute-start(f32[512,1]{0,1:T(1,128)S(1)} %slice_add_fusion), channel_id=1, source_target_pairs={{16,0},{32,16},{48,32},{64,48},{80,64},{96,80},{112,96},{128,112},... | collective-permute-start | bytes 6152 | tf_op jit(solution)/shard_map/ppermute | solution.py:23
Sparse Core Ops, SparseCore 0:
  9.4 46.8 all-gather.3
  58.4 30.7 all-gather.5
